TPU v7x, 32 devices: a whole 2x2x4 slice. The times are simulated.
32 devices in a mesh: blk: 16 (over z, y, x), band: 2 (over core).
Axes of the slice: x: 2, y: 2, z: 4, core: 2. Of those that a mesh axis runs over, the one named last changes fastest.
Arguments:
- traces: bfloat16 [1024, 2, 8192], P('blk', None, 'band'), may hold values from -80 to 80
- sources: bfloat16 [32, 2, 8192], P('blk', None, 'band'), may hold values from -80 to 80
- owner: int32 [1024, 1], P('blk'), may hold values from 0 to 15; in each aligned block of 64 rows (0 to 63, 64 to 127, ...) at most 8 rows name the same one
Outputs:
- gathers: float32 [32, 4, 128, 256], P('blk', None, 'band')
Inputs may be any that keep to these rules, and one draw needn't show every extreme that they name: Among the 64 stations of one device's rows, at most 8 name the same owner block, and some owner block is named by exactly 8 of them in every draw.
All inputs are finite; a program needn't handle non-finite values.
Results may differ from a plain program's by a relative error of at most 0.017.
Values may be sent and summed in bfloat16 or wider, within the bound.
No kernel may reach another device: no remote copies, remote signals or barrier semaphores. Data moves between devices by JAX's collectives and lax.ppermute only.
A program may use at most 128 MiB of HBM per device.

v0:
```python
import math
import jax
import jax.numpy as jnp
from jax import lax
from jax.sharding import PartitionSpec as P

BINS = 8192
LAGS = 2048
DEC = 8
PERIOD = BINS // DEC
EPS = 1e-06


def per_device(traces, sources, owner):
    blocks = lax.axis_size("blk")
    station_count = traces.shape[0]
    source_count = sources.shape[0]
    group_bins = traces.shape[2]
    folds = group_bins // PERIOD
    capacity = max(2, 2 * station_count // blocks)
    lags_out = LAGS // DEC
    offsets = blocks // 4
    all_sources = lax.all_gather(sources, "blk", axis=0, tiled=True)
    trace_float = traces.astype(jnp.float32)
    all_source_float = all_sources.astype(jnp.float32)
    trace_power, source_power = lax.psum(
        (
            jnp.sum(trace_float * trace_float, axis=(1, 2)),
            jnp.sum(all_source_float * all_source_float, axis=(1, 2)),
        ),
        "band",
    )
    white_traces = (
        (trace_float * lax.rsqrt(trace_power / (2 * BINS) + EPS)[:, None, None])
        .astype(jnp.bfloat16)
        .reshape(station_count, 2 * group_bins)
    )
    white_sources = (
        (all_source_float * lax.rsqrt(source_power / (2 * BINS) + EPS)[:, None, None])
        .astype(jnp.bfloat16)
        .astype(jnp.float32)
        .reshape(blocks, source_count, 2, folds, PERIOD)
    )
    owners = owner[:, 0]
    owner_hits = (owners[:, None] == jnp.arange(blocks, dtype=jnp.int32)[None, :]).astype(jnp.int32)
    earlier = jnp.cumsum(owner_hits, axis=0) - owner_hits
    arrival = jnp.sum(owner_hits * earlier, axis=1)
    slot_index = owners * capacity + arrival
    placing = (
        jnp.arange(blocks * capacity, dtype=jnp.int32)[:, None] == slot_index[None, :]
    ).astype(jnp.bfloat16)
    placed = jnp.dot(placing, white_traces, preferred_element_type=jnp.float32)
    placed = placed.reshape(blocks, capacity, 2, folds, PERIOD)
    bin_index = jnp.arange(PERIOD, dtype=jnp.int32)
    lag_value = (jnp.arange(lags_out, dtype=jnp.int32) - lags_out // 2) * DEC
    phase_angle = jnp.mod(bin_index[:, None] * lag_value[None, :], BINS).astype(jnp.float32) * (
        2.0 * math.pi / BINS
    )
    table = jnp.concatenate([jnp.cos(phase_angle), jnp.sin(phase_angle)], axis=0).astype(
        jnp.bfloat16
    )
    norm_scale = BINS ** (-0.5)
    real_s = white_sources[:, None, :, 0]
    imag_s = white_sources[:, None, :, 1]
    cross = []
    for offset in range(offsets):
        visiting = jnp.roll(placed, offset, axis=0)
        real_t = visiting[:, :, None, 0]
        imag_t = visiting[:, :, None, 1]
        even = jnp.sum(real_t * real_s + imag_t * imag_s, axis=3)
        odd = jnp.sum(real_t * imag_s - imag_t * real_s, axis=3)
        cross.append(jnp.concatenate([even, odd], axis=-1))
    cross = jnp.stack(cross, axis=1).astype(jnp.bfloat16)
    rows = blocks * offsets * capacity * source_count
    partial = jnp.dot(cross.reshape(rows, 2 * PERIOD), table, preferred_element_type=jnp.float32)
    partial = (partial * norm_scale).astype(jnp.bfloat16)
    partial = partial.reshape(blocks, offsets, capacity, source_count, lags_out)
    arrived = lax.all_to_all(partial, "blk", split_axis=0, concat_axis=0, tiled=True)
    summed = lax.psum_scatter(arrived.astype(jnp.float32), "band", scatter_dimension=0, tiled=True)
    half = summed.shape[0]
    return jnp.transpose(summed, (3, 1, 0, 2, 4)).reshape(
        source_count, offsets, half * capacity, lags_out
    )


def solution(mesh):
    placed = (P("blk", None, "band"), P("blk", None, "band"), P("blk", None))
    return jax.shard_map(
        per_device,
        mesh=mesh,
        in_specs=placed,
        out_specs=P("blk", None, "band", None),
        check_vma=False,
    )
```

profile of v0, /device:TPU:0, one launch (start us, length us, event | category | flops | bytes accessed | tf_op | source)
XLA Modules:
  0.0 150.7 jit_solution(14130566093052021480)
XLA Ops:
  6.5 0.0 copy-start.8
  6.5 0.0 reduce-scatter.2.cloned.1.call-start
  6.5 45.7 %all_gather.3 = bf16[32,2,4096]{2,1,0:T(2,128)(2,1)S(1)} all-gather(bf16[2,2,4096]{2,1,0:T(2,128)(2,1)} %param.4), channel_id=1, replica_groups=mesh['blk'=16,'band'=2] {'blk'}, dimensions={0}, use_global_device_ids=true | all-gather | bytes 557056 | tf_op jit(solution)/shard_map/all_gather | solution.py:23
  52.2 0.0 copy-start.4
  52.2 0.8 copy-done.4
  53.0 0.8 fusion.12
  53.8 2.8 %fusion = f32[64]{0:T(128)S(1)} fusion(bf16[64,2,4096]{2,1,0:T(2,128)(2,1)} %param.3), kind=kLoop, calls=%fused_computation.17 | loop fusion | flops 1572800 | bytes 1048832 | tf_op jit(solution)/shard_map/reduce_sum | solution.py:28
  56.6 2.5 %all-reduce = (f32[32]{0:T(128)S(1)}, f32[64]{0:T(128)S(1)}) all-reduce(f32[32]{0:T(128)S(1)} %fusion.12, f32[64]{0:T(128)S(1)} %fusion), channel_id=1, replica_groups=mesh['blk'=16,'band'=2] {'band'}, use_global_device_ids=true, to_apply=%region_5.6 | all-reduce | flops 96 | bytes 768 | tf_op jit(solution)/shard_map/psum | solution.py:26
  59.1 2.5 %fusion.1 = bf16[64,2,4096]{2,1,0:T(2,128)(2,1)S(1)} fusion(bf16[64,2,4096]{2,1,0:T(2,128)(2,1)} %param.3, f32[64]{0:T(128)S(1)} %add_rsqrt_fusion.1), kind=kLoop, calls=%fused_computation.18 | loop fusion | flops 1572864 | bytes 2097408 | tf_op jit(solution)/shard_map/convert_element_type | solution.py:35
  61.6 0.6 copy.44
  62.2 0.0 copy-done.8
  62.2 0.1 fusion.26
  62.3 0.1 reduce_window_sum.11
  62.4 0.2 select_reduce_fusion
  62.6 0.7 fusion.24
  63.3 0.2 slice.107
  63.5 0.9 slice.106
  64.5 2.1 %slice.103 = f32[112,8192]{1,0:T(8,128)} slice(f32[128,8192]{1,0:T(8,128)S(1)} %fusion.24), slice={[0:112], [0:8192]} | slice | bytes 7340032 | tf_op jit(solution)/shard_map/jit(_roll_static)/slice | solution.py:67
  66.6 0.8 slice.102
  67.4 2.1 %slice.99 = f32[120,8192]{1,0:T(8,128)} slice(f32[128,8192]{1,0:T(8,128)S(1)} %fusion.24), slice={[0:120], [0:8192]} | slice | bytes 7864320 | tf_op jit(solution)/shard_map/jit(_roll_static)/slice | solution.py:67
  69.6 0.7 slice.98
  70.3 0.0 copy-start.5
  70.3 2.4 %slice_bitcast_fusion.1 = (f32[16,8,4,1024]{3,1,2,0:T(8,128)}, f32[16,8,4,1024]{3,1,2,0:T(8,128)}) fusion(f32[16,8,2,4,1024]{4,1,3,2,0:T(8,128)S(1)} %bitcast.46), kind=kLoop, calls=%fused_computation.32 | loop fusion | bytes 8388608 | tf_op jit(solution)/shard_map/mul | solution.py:70
  72.7 0.0 copy-done.5
  72.7 1.5 %fusion.23 = f32[32,2,4096]{2,1,0:T(2,128)} fusion(f32[32]{0:T(128)S(1)} %add_rsqrt_fusion, bf16[32,2,4096]{2,1,0:T(2,128)(2,1)S(1)} %copy-done.5), kind=kLoop, calls=%fused_computation.57 | loop fusion | flops 1048576 | bytes 1572992 | tf_op jit(solution)/shard_map/reshape | solution.py:42
  74.2 3.3 %reshape.51 = f32[16,2,2,4,1024]{4,3,2,1,0:T(4,128)} reshape(f32[32,2,4096]{2,1,0:T(2,128)} %fusion.23) | data formatting | bytes 2097152 | tf_op jit(solution)/shard_map/reshape | solution.py:42
  77.6 1.3 slice_bitcast_fusion.3
  78.9 0.0 copy-start.1
  78.9 0.0 copy-start.6
  78.9 1.6 %fusion.3 = (f32[16,8,4,1024]{3,1,2,0:T(8,128)S(1)}, f32[16,8,4,1024]{3,1,2,0:T(8,128)S(1)}) fusion(f32[3,8,2,4,1024]{4,1,3,2,0:T(8,128)} %bitcast.52, f32[13,8,2,4,1024]{4,1,3,2,0:T(8,128)S(1)} %bitcast.49), kind=kLoop, calls=%fused_computation.20 | loop fusion | flops 1048576 | bytes 8388608 | tf_op jit(solution)/shard_map/mul | solution.py:70
  80.5 0.6 copy-done.1
  81.2 0.1 copy-done.6
  81.3 0.0 copy-start
  81.3 0.0 copy-start.7
  81.3 0.5 fusion.5
  81.8 1.6 %copy-done = f32[120,8192]{1,0:T(8,128)S(1)} copy-done((f32[120,8192]{1,0:T(8,128)S(1)}, f32[120,8192]{1,0:T(8,128)}, u32[]{:S(2)}) %copy-start) | copy-done | bytes 3932184
  83.4 0.0 copy-done.7
  83.4 0.0 copy-start.2
  83.4 0.0 copy-start.3
  83.4 0.5 fusion.7
  83.9 1.1 copy-done.2
  85.0 0.6 copy-done.3
  85.6 7.3 %add_reduce_fusion.3 = (bf16[16,8,2,1024]{3,1,2,0:T(8,128)(2,1)S(1)}, bf16[16,8,2,1024]{3,1,2,0:T(8,128)(2,1)S(1)}, bf16[16,8,2,1024]{3,1,2,0:T(8,128)(2,1)S(1)}...) fusion(f32[16,2,4,1024]{3,2,1,0:T(4,128)S(1)} %get-tuple-elemen, ...), kind=kLoop, calls=%fused_computation.14 | loop fusion | flops 31457280 | bytes 22020096 | tf_op jit(solution)/shard_map/reduce_sum | solution.py:70
  92.9 0.2 maximum_bitcast_fusion
  93.1 0.2 maximum_bitcast_fusion.2
  93.3 0.6 pad_maximum_fusion
  93.9 6.3 %copy.41 = bf16[16,4,8,2,2048]{4,3,2,1,0:T(2,128)(2,1)} copy(bf16[16,4,8,2,2048]{4,2,3,0,1:T(8,128)(2,1)S(1)} %pad_maximum_fusion) | data formatting | bytes 8388608 | tf_op jit(solution)/shard_map/stack | solution.py:73
  100.2 7.2 %convert_element_type.39 = bf16[1024,2048]{1,0:T(8,128)(2,1)} reshape(bf16[16,4,8,2,2048]{4,3,2,1,0:T(2,128)(2,1)} %copy.41) | data formatting | bytes 8388608 | tf_op jit(solution)/shard_map/convert_element_type | solution.py:73
  107.4 4.4 %cosine_convert_fusion = (bf16[1024,256]{1,0:T(8,128)(2,1)S(1)}, bf16[1024,256]{1,0:T(8,128)(2,1)S(1)}) fusion(s32[256]{0:T(256)S(1)} %add_multiply_fusion), kind=kLoop, calls=%fused_computation.53 | loop fusion | flops 4194304 | bytes 1049600 | tf_op jit(solution)/shard_map/convert.1
  111.8 3.4 %fusion.11 = bf16[1024,256]{1,0:T(8,128)(2,1)S(1)} fusion(bf16[1024,2048]{1,0:T(8,128)(2,1)} %convert_element_type.39, bf16[1024,256]{1,0:T(8,128)(2,1)S(1)} %get-tuple-element.32, bf16[1024,256]{1,0:T(8,128)(2,1)S(1)} %get-tuple-element.31), kind=kOutput, calls=%fused_computation.39 | convolution fusion | flops 1076363264 | bytes 5767168 | tf_op jit(solution)/shard_map/dot_general | solution.py:75
  115.2 0.2 reshape.48
  115.4 0.1 copy.42
  115.5 18.1 %all_to_all.5 = bf16[16,4,8,2,256]{4,2,3,1,0:T(8,128)(2,1)S(1)} all-to-all(bf16[16,4,8,2,256]{4,2,3,1,0:T(8,128)(2,1)S(1)} %copy.42), channel_id=1, replica_groups=mesh['blk'=16,'band'=2] {'blk'}, dimensions={0} | all-to-all | bytes 1048576 | tf_op jit(solution)/shard_map/all_to_all | solution.py:78
  133.6 1.1 convert_element_type.42
  134.7 0.0 reduce-scatter.2.cloned.1.call-update
  134.8 7.2 %reduce-scatter.2.cloned.1.call-done = f32[8,4,8,2,256]{4,2,3,1,0:T(8,128)} async-done(((f32[16,4,8,2,256]{4,2,3,1,0:T(8,128)}), f32[8,4,8,2,256]{4,2,3,1,0:T(8,128)}) %reduce-scatter.2.cloned.1.call-update) | async-done | bytes 524304 | tf_op jit(solution)/shard_map/reduce_scatter | solution.py:79
  142.0 1.9 %copy.46 = f32[8,4,8,2,256]{4,2,0,1,3:T(8,128)} copy(f32[8,4,8,2,256]{4,2,3,1,0:T(8,128)} %reduce-scatter.2.cloned.1.call-done) | data formatting | bytes 1048576 | tf_op jit(solution)/shard_map/reduce_scatter | solution.py:79
  (4 shorter events, 0.0 us)
Async XLA Ops:
  6.5 55.7 %copy-start.8 = (s32[64,1]{0,1:T(1,128)S(1)}, s32[64,1]{0,1:T(1,128)}, u32[]{:S(2)}) copy-start(s32[64,1]{0,1:T(1,128)} %param.5) | copy-start | bytes 772
  6.5 135.4 %reduce-scatter.2.cloned.1.call-start = ((), (), s32[]{:S(2)}) async-start(), calls=%async_computation.2 | async-start | bytes 1572864 | tf_op jit(solution)/shard_map/reduce_scatter | solution.py:79
  52.2 0.8 copy-start.4
  70.3 2.4 %copy-start.5 = (bf16[32,2,4096]{2,1,0:T(2,128)(2,1)S(1)}, bf16[32,2,4096]{2,1,0:T(2,128)(2,1)}, u32[]{:S(2)}) copy-start(bf16[32,2,4096]{2,1,0:T(2,128)(2,1)} %copy-done.4) | copy-start | bytes 1572868
  78.9 2.3 %copy-start.1 = (f32[112,8192]{1,0:T(8,128)S(1)}, f32[112,8192]{1,0:T(8,128)}, u32[]{:S(2)}) copy-start(f32[112,8192]{1,0:T(8,128)} %slice.103) | copy-start | bytes 11010052
  78.9 2.4 %copy-start.6 = (f32[16,8192]{1,0:T(8,128)S(1)}, f32[16,8192]{1,0:T(8,128)}, u32[]{:S(2)}) copy-start(f32[16,8192]{1,0:T(8,128)} %slice.102) | copy-start | bytes 1572868
  81.3 2.1 %copy-start = (f32[120,8192]{1,0:T(8,128)S(1)}, f32[120,8192]{1,0:T(8,128)}, u32[]{:S(2)}) copy-start(f32[120,8192]{1,0:T(8,128)} %slice.99) | copy-start | bytes 11796484
  81.3 2.1 %copy-start.7 = (f32[8,8192]{1,0:T(8,128)S(1)}, f32[8,8192]{1,0:T(8,128)}, u32[]{:S(2)}) copy-start(f32[8,8192]{1,0:T(8,128)} %slice.98) | copy-start | bytes 786436
  83.4 1.6 %copy-start.2 = (f32[16,8,4,1024]{3,1,2,0:T(8,128)S(1)}, f32[16,8,4,1024]{3,1,2,0:T(8,128)}, u32[]{:S(2)}) copy-start(f32[16,8,4,1024]{3,1,2,0:T(8,128)} %get-tuple-element.27) | copy-start | bytes 6291460
  83.4 2.2 %copy-start.3 = (f32[16,8,4,1024]{3,1,2,0:T(8,128)S(1)}, f32[16,8,4,1024]{3,1,2,0:T(8,128)}, u32[]{:S(2)}) copy-start(f32[16,8,4,1024]{3,1,2,0:T(8,128)} %get-tuple-element.28) | copy-start | bytes 6291460
Sparse Core Ops, SparseCore 0:
  134.9 7.0 reduce-scatter.1
where the time goes:
time: 151 us
  blocking collectives  66.2 us (44%)
  local copies, waits for them, and re-layouts  35.1 us (23%)
  other arithmetic  24.5 us (16%)
  between operations  13.6 us (9%)
  waiting for transfers between devices  7.22 us (5%)
  matrix products  4.13 us (3%)
    all_gather x1, blocking collectives, per_device(): all_sources = lax.all_gather(sources, 'blk', axis=0, tiled=True)  45.7 us
    all_to_all x1, blocking collectives, per_device(): lax.all_to_all(partial, 'blk', split_axis=0, concat_axis=0, tiled=True)  18.1 us
    reduce_sum x1, other arithmetic, per_device(): even = jnp.sum(real_t * real_s + imag_t * imag_s, axis=3)  7.3 us
    reduce_scatter x1, waiting for transfers between devices, per_device(): lax.psum_scatter(arrived.astype(jnp.float32), 'band', scatter_dimension=0...  7.2 us
    convert_element_type x1, local copies, waits for them, and re-layouts, per_device(): cross = jnp.stack(cross, axis=1).astype(jnp.bfloat16)  7.2 us
    slice x6, local copies, waits for them, and re-layouts, per_device(): visiting = jnp.roll(placed, offset, axis=0)  6.99 us
    another operation x1, local copies, waits for them, and re-layouts, per_device(): cross = jnp.stack(cross, axis=1).astype(jnp.bfloat16)  6.3 us
    unnamed x19, local copies, waits for them, and re-layouts  5.42 us
  transfers between devices with their start and end apart: 1, of which 1 were waited for; matrix products, arithmetic and copies ran while one was open for 0% of the time, Pallas kernels for 0%

commit v1 on v0

--- a/solution.py
+++ b/solution.py
@@ -75,7 +75,19 @@
     partial = jnp.dot(cross.reshape(rows, 2 * PERIOD), table, preferred_element_type=jnp.float32)
     partial = (partial * norm_scale).astype(jnp.bfloat16)
     partial = partial.reshape(blocks, offsets, capacity, source_count, lags_out)
-    arrived = lax.all_to_all(partial, "blk", split_axis=0, concat_axis=0, tiled=True)
+    r_now, w_next = (lax.axis_size("blk"), lax.axis_index("blk"))
+    aux = partial.shape[0] // r_now
+    t1 = jnp.roll(partial, -w_next * aux, 0)
+    inbox = [lax.slice_in_dim(t1, 0, aux, axis=0)]
+    nth = 1
+    while nth < r_now:
+        x_new = lax.slice_in_dim(t1, nth * aux, (nth + 1) * aux, axis=0)
+        inbox.append(
+            lax.ppermute(x_new, "blk", [(num, (num + nth) % r_now) for num in range(r_now)])
+        )
+        nth = nth + 1
+    q_next = jnp.concatenate(inbox[::-1], axis=0)
+    arrived = jnp.roll(q_next, shift=(w_next + 1) * inbox[0].shape[0], axis=0)
     summed = lax.psum_scatter(arrived.astype(jnp.float32), "band", scatter_dimension=0, tiled=True)
     half = summed.shape[0]
     return jnp.transpose(summed, (3, 1, 0, 2, 4)).reshape(

time: 151 us -> 164 us (1.086)
  starting transfers between devices: 0.01 us -> 20.7 us
  blocking collectives: 66.2 us -> 48.1 us
  waiting for transfers between devices: 7.22 us -> 13.6 us
  local copies, waits for them, and re-layouts: 35.1 us -> 38 us
    ppermute x0 -> x15, starting transfers between devices: none -> 20.7 us  [per_device(): lax.ppermute(x_new, 'blk', [(num, (num + nth) % r_now) for num in range(r...]
    all_to_all x1 -> x0, blocking collectives: 18.1 us -> none  [per_device(): lax.all_to_all(partial, 'blk', split_axis=0, concat_axis=0, tiled=True)]
    ppermute x0 -> x15, waiting for transfers between devices: none -> 6.59 us  [per_device(): lax.ppermute(x_new, 'blk', [(num, (num + nth) % r_now) for num in range(r...]
    mul x2, local copies, waits for them, and re-layouts: 3.67 us -> 6.21 us  [per_device(): even = jnp.sum(real_t * real_s + imag_t * imag_s, axis=3)]
    unnamed x19 -> x36, local copies, waits for them, and re-layouts: 5.42 us -> 5.48 us
  transfers between devices with their start and end apart: 1 -> 16, of which waited for: 1 -> 6; matrix products, arithmetic and copies ran while one was open for 0% -> 0% of each run, Pallas kernels for 0% -> 0%
where the time goes in v1:
time: 164 us; the launch traced here: 163 us
  blocking collectives  48.1 us (29%)
  local copies, waits for them, and re-layouts  38 us (23%)
  other arithmetic  24.8 us (15%)
  starting transfers between devices  20.7 us (13%)
  between operations  13.7 us (8%)
  waiting for transfers between devices  13.6 us (8%)
  matrix products  4.13 us (3%)
    all_gather x1, blocking collectives, per_device(): all_sources = lax.all_gather(sources, 'blk', axis=0, tiled=True)  45.7 us
    ppermute x15, starting transfers between devices, per_device(): lax.ppermute(x_new, 'blk', [(num, (num + nth) % r_now) for num in range(r...  20.7 us
    reduce_sum x1, other arithmetic, per_device(): even = jnp.sum(real_t * real_s + imag_t * imag_s, axis=3)  7.3 us
    slice x6, local copies, waits for them, and re-layouts, per_device(): visiting = jnp.roll(placed, offset, axis=0)  7.26 us
    convert_element_type x1, local copies, waits for them, and re-layouts, per_device(): cross = jnp.stack(cross, axis=1).astype(jnp.bfloat16)  7.2 us
    reduce_scatter x1, waiting for transfers between devices, per_device(): lax.psum_scatter(arrived.astype(jnp.float32), 'band', scatter_dimension=0...  6.95 us
    ppermute x15, waiting for transfers between devices, per_device(): lax.ppermute(x_new, 'blk', [(num, (num + nth) % r_now) for num in range(r...  6.59 us
    another operation x1, local copies, waits for them, and re-layouts, per_device(): cross = jnp.stack(cross, axis=1).astype(jnp.bfloat16)  6.3 us
  transfers between devices with their start and end apart: 16, of which 6 were waited for; matrix products, arithmetic and copies ran while one was open for 0% of the time, Pallas kernels for 0%

profile of v1, /device:TPU:0, one launch (start us, length us, event | category | flops | bytes accessed | tf_op | source)
XLA Modules:
  0.0 163.0 jit_solution(17361109270526813846)
XLA Ops:
  6.5 45.7 %all_gather.3 = bf16[32,2,4096]{2,1,0:T(2,128)(2,1)S(1)} all-gather(bf16[2,2,4096]{2,1,0:T(2,128)(2,1)} %param.6), channel_id=1, replica_groups=mesh['blk'=16,'band'=2] {'blk'}, dimensions={0}, use_global_device_ids=true | all-gather | bytes 557056 | tf_op jit(solution)/shard_map/all_gather | solution.py:23
  52.2 0.8 copy-done.5
  53.0 0.8 fusion.12
  53.8 2.8 %fusion = f32[64]{0:T(128)S(1)} fusion(bf16[64,2,4096]{2,1,0:T(2,128)(2,1)} %param.5), kind=kLoop, calls=%fused_computation.17 | loop fusion | flops 1572800 | bytes 1048832 | tf_op jit(solution)/shard_map/reduce_sum | solution.py:28
  56.6 2.5 %all-reduce = (f32[32]{0:T(128)S(1)}, f32[64]{0:T(128)S(1)}) all-reduce(f32[32]{0:T(128)S(1)} %fusion.12, f32[64]{0:T(128)S(1)} %fusion), channel_id=1, replica_groups=mesh['blk'=16,'band'=2] {'band'}, use_global_device_ids=true, to_apply=%region_5.6 | all-reduce | flops 96 | bytes 768 | tf_op jit(solution)/shard_map/psum | solution.py:26
  59.1 2.5 %fusion.1 = bf16[64,2,4096]{2,1,0:T(2,128)(2,1)S(1)} fusion(bf16[64,2,4096]{2,1,0:T(2,128)(2,1)} %param.5, f32[64]{0:T(128)S(1)} %add_rsqrt_fusion.1), kind=kLoop, calls=%fused_computation.18 | loop fusion | flops 1572864 | bytes 2097408 | tf_op jit(solution)/shard_map/convert_element_type | solution.py:35
  61.6 0.6 copy.47
  62.2 0.1 fusion.29
  62.3 0.1 reduce_window_sum.11
  62.4 0.2 select_reduce_fusion
  62.6 0.7 fusion.27
  63.3 0.2 slice.171
  63.6 1.2 slice.170
  64.7 2.2 %slice.167 = f32[112,8192]{1,0:T(8,128)} slice(f32[128,8192]{1,0:T(8,128)S(1)} %fusion.27), slice={[0:112], [0:8192]} | slice | bytes 7340032 | tf_op jit(solution)/shard_map/jit(_roll_static)/slice | solution.py:67
  66.9 0.8 slice.166
  67.7 2.2 %slice.163 = f32[120,8192]{1,0:T(8,128)} slice(f32[128,8192]{1,0:T(8,128)S(1)} %fusion.27), slice={[0:120], [0:8192]} | slice | bytes 7864320 | tf_op jit(solution)/shard_map/jit(_roll_static)/slice | solution.py:67
  69.9 0.7 slice.162
  70.6 4.9 %slice_bitcast_fusion.1 = (f32[16,8,4,1024]{3,1,2,0:T(8,128)}, f32[16,8,4,1024]{3,1,2,0:T(8,128)}) fusion(f32[16,8,2,4,1024]{4,1,3,2,0:T(8,128)} %bitcast.46), kind=kLoop, calls=%fused_computation.32 | loop fusion | bytes 8388608 | tf_op jit(solution)/shard_map/mul | solution.py:70
  75.5 1.5 fusion.23
  77.0 3.3 %reshape.51 = f32[16,2,2,4,1024]{4,3,2,1,0:T(4,128)} reshape(f32[32,2,4096]{2,1,0:T(2,128)} %fusion.23) | data formatting | bytes 2097152 | tf_op jit(solution)/shard_map/reshape | solution.py:42
  80.4 1.3 slice_bitcast_fusion.3
  81.7 1.6 fusion.3
  83.3 0.6 copy-done.2
  84.0 0.1 copy-done.7
  84.1 0.5 fusion.5
  84.6 1.6 copy-done.1
  86.2 0.0 copy-done.8
  86.2 0.5 fusion.7
  86.7 1.1 copy-done.3
  87.8 0.6 copy-done.4
  88.4 7.3 %add_reduce_fusion.3 = (bf16[16,8,2,1024]{3,1,2,0:T(8,128)(2,1)S(1)}, bf16[16,8,2,1024]{3,1,2,0:T(8,128)(2,1)S(1)}, bf16[16,8,2,1024]{3,1,2,0:T(8,128)(2,1)S(1)}...) fusion(f32[16,2,4,1024]{3,2,1,0:T(4,128)S(1)} %get-tuple-elemen, ...), kind=kLoop, calls=%fused_computation.14 | loop fusion | flops 31457280 | bytes 22020096 | tf_op jit(solution)/shard_map/reduce_sum | solution.py:70
  95.7 0.2 maximum_bitcast_fusion
  95.9 0.2 maximum_bitcast_fusion.2
  96.1 0.6 pad_maximum_fusion
  96.7 6.3 %copy.43 = bf16[16,4,8,2,2048]{4,3,2,1,0:T(2,128)(2,1)} copy(bf16[16,4,8,2,2048]{4,2,3,0,1:T(8,128)(2,1)S(1)} %pad_maximum_fusion) | data formatting | bytes 8388608 | tf_op jit(solution)/shard_map/stack | solution.py:73
  103.0 7.2 %convert_element_type.39 = bf16[1024,2048]{1,0:T(8,128)(2,1)} reshape(bf16[16,4,8,2,2048]{4,3,2,1,0:T(2,128)(2,1)} %copy.43) | data formatting | bytes 8388608 | tf_op jit(solution)/shard_map/convert_element_type | solution.py:73
  110.2 4.4 %cosine_convert_fusion = (bf16[1024,256]{1,0:T(8,128)(2,1)S(1)}, bf16[1024,256]{1,0:T(8,128)(2,1)S(1)}) fusion(s32[256]{0:T(256)S(1)} %add_multiply_fusion), kind=kLoop, calls=%fused_computation.57 | loop fusion | flops 4194304 | bytes 1049600 | tf_op jit(solution)/shard_map/convert.1
  114.6 3.4 %fusion.11 = bf16[1024,256]{1,0:T(8,128)(2,1)S(1)} fusion(bf16[1024,2048]{1,0:T(8,128)(2,1)} %convert_element_type.39, bf16[1024,256]{1,0:T(8,128)(2,1)S(1)} %get-tuple-element.48, bf16[1024,256]{1,0:T(8,128)(2,1)S(1)} %get-tuple-element.47), kind=kOutput, calls=%fused_computation.39 | convolution fusion | flops 1076363264 | bytes 5767168 | tf_op jit(solution)/shard_map/dot_general | solution.py:75
  118.0 0.2 reshape.48
  118.2 0.1 copy.44
  118.4 0.2 fusion.26
  118.6 0.1 collective-permute-start
  118.7 0.1 collective-permute-start.1
  118.8 0.1 collective-permute-start.2
  118.8 0.1 collective-permute-start.3
  118.9 3.5 %collective-permute-start.4 = (bf16[1,4,8,2,256]{4,2,3,1,0:T(8,128)(2,1)S(1)}, bf16[1,4,8,2,256]{4,2,3,1,0:T(8,128)(2,1)S(1)}, u32[]{:S(2)}, u32[]{:S(2)}) collective-permute-start(bf16[1,4,8,2,256]{4,2,3,1,0:T(8,128)(2,1)S(1)} %get-tuple-element.42), channel_id=1, source_target_pairs={{0,22},{2,24},{4,26},{6,28},{8,30},{10,0},{12,2},{14,4},{16,6},{18... | collective-permute-start | bytes 98312 | tf_op jit(solution)/shard_map/ppermute | solution.py:86
  122.3 0.2 collective-permute-done
  122.6 2.9 %collective-permute-start.5 = (bf16[1,4,8,2,256]{4,2,3,1,0:T(8,128)(2,1)S(1)}, bf16[1,4,8,2,256]{4,2,3,1,0:T(8,128)(2,1)S(1)}, u32[]{:S(2)}, u32[]{:S(2)}) collective-permute-start(bf16[1,4,8,2,256]{4,2,3,1,0:T(8,128)(2,1)S(1)} %get-tuple-element.41), channel_id=1, source_target_pairs={{0,20},{2,22},{4,24},{6,26},{8,28},{10,30},{12,0},{14,2},{16,4},{1... | collective-permute-start | bytes 98312 | tf_op jit(solution)/shard_map/ppermute | solution.py:86
  125.5 0.0 collective-permute-done.1
  125.5 3.4 %collective-permute-start.7 = (bf16[1,4,8,2,256]{4,2,3,1,0:T(8,128)(2,1)S(1)}, bf16[1,4,8,2,256]{4,2,3,1,0:T(8,128)(2,1)S(1)}, u32[]{:S(2)}, u32[]{:S(2)}) collective-permute-start(bf16[1,4,8,2,256]{4,2,3,1,0:T(8,128)(2,1)S(1)} %get-tuple-element.39), channel_id=1, source_target_pairs={{0,16},{2,18},{4,20},{6,22},{8,24},{10,26},{12,28},{14,30},{16,0},... | collective-permute-start | bytes 98312 | tf_op jit(solution)/shard_map/ppermute | solution.py:86
  128.9 0.5 collective-permute-start.8
  129.4 2.9 %collective-permute-start.9 = (bf16[1,4,8,2,256]{4,2,3,1,0:T(8,128)(2,1)S(1)}, bf16[1,4,8,2,256]{4,2,3,1,0:T(8,128)(2,1)S(1)}, u32[]{:S(2)}, u32[]{:S(2)}) collective-permute-start(bf16[1,4,8,2,256]{4,2,3,1,0:T(8,128)(2,1)S(1)} %get-tuple-element.37), channel_id=1, source_target_pairs={{0,12},{2,14},{4,16},{6,18},{8,20},{10,22},{12,24},{14,26},{16,28}... | collective-permute-start | bytes 98312 | tf_op jit(solution)/shard_map/ppermute | solution.py:86
  132.3 1.9 %collective-permute-start.10 = (bf16[1,4,8,2,256]{4,2,3,1,0:T(8,128)(2,1)S(1)}, bf16[1,4,8,2,256]{4,2,3,1,0:T(8,128)(2,1)S(1)}, u32[]{:S(2)}, u32[]{:S(2)}) collective-permute-start(bf16[1,4,8,2,256]{4,2,3,1,0:T(8,128)(2,1)S(1)} %get-tuple-element.36), channel_id=1, source_target_pairs={{0,10},{2,12},{4,14},{6,16},{8,18},{10,20},{12,22},{14,24},{16,26}... | collective-permute-start | bytes 98312 | tf_op jit(solution)/shard_map/ppermute | solution.py:86
  134.3 1.0 collective-permute-start.11
  135.2 3.3 %collective-permute-start.12 = (bf16[1,4,8,2,256]{4,2,3,1,0:T(8,128)(2,1)S(1)}, bf16[1,4,8,2,256]{4,2,3,1,0:T(8,128)(2,1)S(1)}, u32[]{:S(2)}, u32[]{:S(2)}) collective-permute-start(bf16[1,4,8,2,256]{4,2,3,1,0:T(8,128)(2,1)S(1)} %get-tuple-element.34), channel_id=1, source_target_pairs={{0,6},{2,8},{4,10},{6,12},{8,14},{10,16},{12,18},{14,20},{16,22},{... | collective-permute-start | bytes 98312 | tf_op jit(solution)/shard_map/ppermute | solution.py:86
  138.5 1.2 collective-permute-start.14
  139.8 0.2 collective-permute-done.11
  140.0 3.1 %collective-permute-done.12 = bf16[1,4,8,2,256]{4,2,3,1,0:T(8,128)(2,1)S(1)} collective-permute-done((bf16[1,4,8,2,256]{4,2,3,1,0:T(8,128)(2,1)S(1)}, bf16[1,4,8,2,256]{4,2,3,1,0:T(8,128)(2,1)S(1)}, u32[]{:S(2)}, u32[]{:S(2)}) %collective-permute-start.12) | collective-permute-done | bytes 32800 | tf_op jit(solution)/shard_map/ppermute | solution.py:86
  143.1 2.0 %collective-permute-done.13 = bf16[1,4,8,2,256]{4,2,3,1,0:T(8,128)(2,1)S(1)} collective-permute-done((bf16[1,4,8,2,256]{4,2,3,1,0:T(8,128)(2,1)S(1)}, bf16[1,4,8,2,256]{4,2,3,1,0:T(8,128)(2,1)S(1)}, u32[]{:S(2)}, u32[]{:S(2)}) %collective-permute-start.13) | collective-permute-done | bytes 32800 | tf_op jit(solution)/shard_map/ppermute | solution.py:86
  145.1 1.0 collective-permute-done.14
  146.1 1.2 fusion.25
  147.3 0.0 reduce-scatter.2.cloned.1.call-update
  147.4 7.0 %reduce-scatter.2.cloned.1.call-done = f32[8,4,8,2,256]{4,2,3,1,0:T(8,128)} async-done(((f32[16,4,8,2,256]{4,2,3,1,0:T(8,128)}), f32[8,4,8,2,256]{4,2,3,1,0:T(8,128)}) %reduce-scatter.2.cloned.1.call-update) | async-done | bytes 524304 | tf_op jit(solution)/shard_map/reduce_scatter | solution.py:91
  154.3 1.9 %copy.49 = f32[8,4,8,2,256]{4,2,0,1,3:T(8,128)} copy(f32[8,4,8,2,256]{4,2,3,1,0:T(8,128)} %reduce-scatter.2.cloned.1.call-done) | data formatting | bytes 1048576 | tf_op jit(solution)/shard_map/reduce_scatter | solution.py:91
  (46 shorter events, 0.2 us)
Async XLA Ops:
  6.5 55.7 %copy-start.9 = (s32[64,1]{0,1:T(1,128)S(1)}, s32[64,1]{0,1:T(1,128)}, u32[]{:S(2)}) copy-start(s32[64,1]{0,1:T(1,128)} %param.7) | copy-start | bytes 772
  6.5 147.8 %reduce-scatter.2.cloned.1.call-start = ((), (), s32[]{:S(2)}) async-start(), calls=%async_computation.1 | async-start | bytes 1572864 | tf_op jit(solution)/shard_map/reduce_scatter | solution.py:91
  52.2 0.8 copy-start.5
  63.3 6.6 %copy-start = (f32[128,8192]{1,0:T(8,128)}, f32[128,8192]{1,0:T(8,128)S(1)}, u32[]{:S(2)}) copy-start(f32[128,8192]{1,0:T(8,128)S(1)} %fusion.27) | copy-start | bytes 12582916
  70.6 4.9 %copy-start.6 = (bf16[32,2,4096]{2,1,0:T(2,128)(2,1)S(1)}, bf16[32,2,4096]{2,1,0:T(2,128)(2,1)}, u32[]{:S(2)}) copy-start(bf16[32,2,4096]{2,1,0:T(2,128)(2,1)} %copy-done.5) | copy-start | bytes 1572868
  81.7 2.3 %copy-start.2 = (f32[112,8192]{1,0:T(8,128)S(1)}, f32[112,8192]{1,0:T(8,128)}, u32[]{:S(2)}) copy-start(f32[112,8192]{1,0:T(8,128)} %slice.167) | copy-start | bytes 11010052
  81.7 2.4 %copy-start.7 = (f32[16,8192]{1,0:T(8,128)S(1)}, f32[16,8192]{1,0:T(8,128)}, u32[]{:S(2)}) copy-start(f32[16,8192]{1,0:T(8,128)} %slice.166) | copy-start | bytes 1572868
  84.1 2.1 %copy-start.1 = (f32[120,8192]{1,0:T(8,128)S(1)}, f32[120,8192]{1,0:T(8,128)}, u32[]{:S(2)}) copy-start(f32[120,8192]{1,0:T(8,128)} %slice.163) | copy-start | bytes 11796484
  84.1 2.1 %copy-start.8 = (f32[8,8192]{1,0:T(8,128)S(1)}, f32[8,8192]{1,0:T(8,128)}, u32[]{:S(2)}) copy-start(f32[8,8192]{1,0:T(8,128)} %slice.162) | copy-start | bytes 786436
  86.2 1.6 copy-start.3
  86.2 2.2 %copy-start.4 = (f32[16,8,4,1024]{3,1,2,0:T(8,128)S(1)}, f32[16,8,4,1024]{3,1,2,0:T(8,128)}, u32[]{:S(2)}) copy-start(f32[16,8,4,1024]{3,1,2,0:T(8,128)} %get-tuple-element.29) | copy-start | bytes 6291460
  118.6 4.0 %collective-permute-start = (bf16[1,4,8,2,256]{4,2,3,1,0:T(8,128)(2,1)S(1)}, bf16[1,4,8,2,256]{4,2,3,1,0:T(8,128)(2,1)S(1)}, u32[]{:S(2)}, u32[]{:S(2)}) collective-permute-start(bf16[1,4,8,2,256]{4,2,3,1,0:T(8,128)(2,1)S(1)} %get-tuple-element.46), channel_id=1, source_target_pairs={{0,30},{2,0},{4,2},{6,4},{8,6},{10,8},{12,10},{14,12},{16,14},{18,... | collective-permute-start | bytes 98312 | tf_op jit(solution)/shard_map/ppermute | solution.py:86
  118.7 6.8 %collective-permute-start.1 = (bf16[1,4,8,2,256]{4,2,3,1,0:T(8,128)(2,1)S(1)}, bf16[1,4,8,2,256]{4,2,3,1,0:T(8,128)(2,1)S(1)}, u32[]{:S(2)}, u32[]{:S(2)}) collective-permute-start(bf16[1,4,8,2,256]{4,2,3,1,0:T(8,128)(2,1)S(1)} %get-tuple-element.45), channel_id=1, source_target_pairs={{0,28},{2,30},{4,0},{6,2},{8,4},{10,6},{12,8},{14,10},{16,12},{18,... | collective-permute-start | bytes 98312 | tf_op jit(solution)/shard_map/ppermute | solution.py:86
  118.8 6.8 %collective-permute-start.2 = (bf16[1,4,8,2,256]{4,2,3,1,0:T(8,128)(2,1)S(1)}, bf16[1,4,8,2,256]{4,2,3,1,0:T(8,128)(2,1)S(1)}, u32[]{:S(2)}, u32[]{:S(2)}) collective-permute-start(bf16[1,4,8,2,256]{4,2,3,1,0:T(8,128)(2,1)S(1)} %get-tuple-element.44), channel_id=1, source_target_pairs={{0,26},{2,28},{4,30},{6,0},{8,2},{10,4},{12,6},{14,8},{16,10},{18,... | collective-permute-start | bytes 98312 | tf_op jit(solution)/shard_map/ppermute | solution.py:86
  118.8 10.1 %collective-permute-start.3 = (bf16[1,4,8,2,256]{4,2,3,1,0:T(8,128)(2,1)S(1)}, bf16[1,4,8,2,256]{4,2,3,1,0:T(8,128)(2,1)S(1)}, u32[]{:S(2)}, u32[]{:S(2)}) collective-permute-start(bf16[1,4,8,2,256]{4,2,3,1,0:T(8,128)(2,1)S(1)} %get-tuple-element.43), channel_id=1, source_target_pairs={{0,24},{2,26},{4,28},{6,30},{8,0},{10,2},{12,4},{14,6},{16,8},{18,... | collective-permute-start | bytes 98312 | tf_op jit(solution)/shard_map/ppermute | solution.py:86
  118.9 10.5 %collective-permute-start.4 = (bf16[1,4,8,2,256]{4,2,3,1,0:T(8,128)(2,1)S(1)}, bf16[1,4,8,2,256]{4,2,3,1,0:T(8,128)(2,1)S(1)}, u32[]{:S(2)}, u32[]{:S(2)}) collective-permute-start(bf16[1,4,8,2,256]{4,2,3,1,0:T(8,128)(2,1)S(1)} %get-tuple-element.42), channel_id=1, source_target_pairs={{0,22},{2,24},{4,26},{6,28},{8,30},{10,0},{12,2},{14,4},{16,6},{18... | collective-permute-start | bytes 98312 | tf_op jit(solution)/shard_map/ppermute | solution.py:86
  122.6 9.8 %collective-permute-start.5 = (bf16[1,4,8,2,256]{4,2,3,1,0:T(8,128)(2,1)S(1)}, bf16[1,4,8,2,256]{4,2,3,1,0:T(8,128)(2,1)S(1)}, u32[]{:S(2)}, u32[]{:S(2)}) collective-permute-start(bf16[1,4,8,2,256]{4,2,3,1,0:T(8,128)(2,1)S(1)} %get-tuple-element.41), channel_id=1, source_target_pairs={{0,20},{2,22},{4,24},{6,26},{8,28},{10,30},{12,0},{14,2},{16,4},{1... | collective-permute-start | bytes 98312 | tf_op jit(solution)/shard_map/ppermute | solution.py:86
  125.5 8.7 %collective-permute-start.6 = (bf16[1,4,8,2,256]{4,2,3,1,0:T(8,128)(2,1)S(1)}, bf16[1,4,8,2,256]{4,2,3,1,0:T(8,128)(2,1)S(1)}, u32[]{:S(2)}, u32[]{:S(2)}) collective-permute-start(bf16[1,4,8,2,256]{4,2,3,1,0:T(8,128)(2,1)S(1)} %get-tuple-element.40), channel_id=1, source_target_pairs={{0,18},{2,20},{4,22},{6,24},{8,26},{10,28},{12,30},{14,0},{16,2},{... | collective-permute-start | bytes 98312 | tf_op jit(solution)/shard_map/ppermute | solution.py:86
  125.5 9.7 %collective-permute-start.7 = (bf16[1,4,8,2,256]{4,2,3,1,0:T(8,128)(2,1)S(1)}, bf16[1,4,8,2,256]{4,2,3,1,0:T(8,128)(2,1)S(1)}, u32[]{:S(2)}, u32[]{:S(2)}) collective-permute-start(bf16[1,4,8,2,256]{4,2,3,1,0:T(8,128)(2,1)S(1)} %get-tuple-element.39), channel_id=1, source_target_pairs={{0,16},{2,18},{4,20},{6,22},{8,24},{10,26},{12,28},{14,30},{16,0},... | collective-permute-start | bytes 98312 | tf_op jit(solution)/shard_map/ppermute | solution.py:86
  128.9 9.6 %collective-permute-start.8 = (bf16[1,4,8,2,256]{4,2,3,1,0:T(8,128)(2,1)S(1)}, bf16[1,4,8,2,256]{4,2,3,1,0:T(8,128)(2,1)S(1)}, u32[]{:S(2)}, u32[]{:S(2)}) collective-permute-start(bf16[1,4,8,2,256]{4,2,3,1,0:T(8,128)(2,1)S(1)} %get-tuple-element.38), channel_id=1, source_target_pairs={{0,14},{2,16},{4,18},{6,20},{8,22},{10,24},{12,26},{14,28},{16,30}... | collective-permute-start | bytes 98312 | tf_op jit(solution)/shard_map/ppermute | solution.py:86
  129.4 9.1 %collective-permute-start.9 = (bf16[1,4,8,2,256]{4,2,3,1,0:T(8,128)(2,1)S(1)}, bf16[1,4,8,2,256]{4,2,3,1,0:T(8,128)(2,1)S(1)}, u32[]{:S(2)}, u32[]{:S(2)}) collective-permute-start(bf16[1,4,8,2,256]{4,2,3,1,0:T(8,128)(2,1)S(1)} %get-tuple-element.37), channel_id=1, source_target_pairs={{0,12},{2,14},{4,16},{6,18},{8,20},{10,22},{12,24},{14,26},{16,28}... | collective-permute-start | bytes 98312 | tf_op jit(solution)/shard_map/ppermute | solution.py:86
  132.3 7.4 %collective-permute-start.10 = (bf16[1,4,8,2,256]{4,2,3,1,0:T(8,128)(2,1)S(1)}, bf16[1,4,8,2,256]{4,2,3,1,0:T(8,128)(2,1)S(1)}, u32[]{:S(2)}, u32[]{:S(2)}) collective-permute-start(bf16[1,4,8,2,256]{4,2,3,1,0:T(8,128)(2,1)S(1)} %get-tuple-element.36), channel_id=1, source_target_pairs={{0,10},{2,12},{4,14},{6,16},{8,18},{10,20},{12,22},{14,24},{16,26}... | collective-permute-start | bytes 98312 | tf_op jit(solution)/shard_map/ppermute | solution.py:86
  134.3 5.7 %collective-permute-start.11 = (bf16[1,4,8,2,256]{4,2,3,1,0:T(8,128)(2,1)S(1)}, bf16[1,4,8,2,256]{4,2,3,1,0:T(8,128)(2,1)S(1)}, u32[]{:S(2)}, u32[]{:S(2)}) collective-permute-start(bf16[1,4,8,2,256]{4,2,3,1,0:T(8,128)(2,1)S(1)} %get-tuple-element.35), channel_id=1, source_target_pairs={{0,8},{2,10},{4,12},{6,14},{8,16},{10,18},{12,20},{14,22},{16,24},... | collective-permute-start | bytes 98312 | tf_op jit(solution)/shard_map/ppermute | solution.py:86
  135.2 7.8 %collective-permute-start.12 = (bf16[1,4,8,2,256]{4,2,3,1,0:T(8,128)(2,1)S(1)}, bf16[1,4,8,2,256]{4,2,3,1,0:T(8,128)(2,1)S(1)}, u32[]{:S(2)}, u32[]{:S(2)}) collective-permute-start(bf16[1,4,8,2,256]{4,2,3,1,0:T(8,128)(2,1)S(1)} %get-tuple-element.34), channel_id=1, source_target_pairs={{0,6},{2,8},{4,10},{6,12},{8,14},{10,16},{12,18},{14,20},{16,22},{... | collective-permute-start | bytes 98312 | tf_op jit(solution)/shard_map/ppermute | solution.py:86
  138.5 6.6 %collective-permute-start.13 = (bf16[1,4,8,2,256]{4,2,3,1,0:T(8,128)(2,1)S(1)}, bf16[1,4,8,2,256]{4,2,3,1,0:T(8,128)(2,1)S(1)}, u32[]{:S(2)}, u32[]{:S(2)}) collective-permute-start(bf16[1,4,8,2,256]{4,2,3,1,0:T(8,128)(2,1)S(1)} %get-tuple-element.33), channel_id=1, source_target_pairs={{0,4},{2,6},{4,8},{6,10},{8,12},{10,14},{12,16},{14,18},{16,20},{1... | collective-permute-start | bytes 98312 | tf_op jit(solution)/shard_map/ppermute | solution.py:86
  138.5 7.6 %collective-permute-start.14 = (bf16[1,4,8,2,256]{4,2,3,1,0:T(8,128)(2,1)S(1)}, bf16[1,4,8,2,256]{4,2,3,1,0:T(8,128)(2,1)S(1)}, u32[]{:S(2)}, u32[]{:S(2)}) collective-permute-start(bf16[1,4,8,2,256]{4,2,3,1,0:T(8,128)(2,1)S(1)} %get-tuple-element.32), channel_id=1, source_target_pairs={{0,2},{2,4},{4,6},{6,8},{8,10},{10,12},{12,14},{14,16},{16,18},{18... | collective-permute-start | bytes 98312 | tf_op jit(solution)/shard_map/ppermute | solution.py:86
Sparse Core Ops, SparseCore 0:
  147.5 6.7 reduce-scatter.1
